TPU v7x, 32 devices: a whole 2x2x4 slice. The times are simulated.
32 devices in a mesh: groups: 2 (over x), date: 8 (over z, y), row: 2 (over core).
Axes of the slice: x: 2, y: 2, z: 4, core: 2. Of those that a mesh axis runs over, the one named last changes fastest.
Arguments:
- scenes: bfloat16 [16, 4, 512, 1024], P(('groups', 'date'), None, 'row'), parts along dimension 0, may hold values from -6 to 6
- resample_taps: float32 [2, 4, 7], replicated, may hold values from 0 to 0.35
- clear_mask: int32 [16, 128, 8], P('groups', ('row', 'date')), parts along dimension 0, may hold values 0 or 1
Outputs:
- smooth_fine: bfloat16 [16, 4, 512, 1024], P('groups', None, ('row', 'date')), parts along dimension 0
- smooth_half: bfloat16 [16, 4, 256, 512], P('groups', None, ('row', 'date')), parts along dimension 0
- smooth_quarter: bfloat16 [16, 4, 128, 256], P('groups', None, ('row', 'date')), parts along dimension 0
There are 2 independent parts, one for each index of `groups`. A program takes and returns all parts, laid end to end along the dimension named above; an argument that names none is the same for every part. Nothing has to cross between parts.
Inputs may be any that keep to these rules, and one draw needn't show every extreme that they name: `clear_mask`: 1 marks a clear block, 0 a cloudy one.
All inputs are finite; a program needn't handle non-finite values.
Results may differ from a plain program's by a relative error of at most 0.005.
Values may be sent and summed in bfloat16 or wider, within the bound.
No kernel may reach another device: no remote copies, remote signals or barrier semaphores. Data moves between devices by JAX's collectives and lax.ppermute only.
A program may use at most 128 MiB of HBM per device.

v0:
```python
import math
import jax
import jax.numpy as jnp
import numpy as np
from jax import lax
from jax.sharding import PartitionSpec as P

gap_weights = [math.exp(-((k - 4) ** 2) / 8.0) for k in range(9)]
savgol_coeffs = [c / 231.0 for c in [-21.0, 14.0, 39.0, 54.0, 59.0, 54.0, 39.0, 14.0, -21.0]]
pyramid_filter = [0.125, 0.375, 0.375, 0.125]


def padded(block, sides, width):
    for axis, dim in sides:
        count = lax.axis_size(axis)
        forward = [(i, i + 1) for i in range(count - 1)]
        backward = [(target, source) for source, target in forward]
        low = lax.ppermute(
            lax.slice_in_dim(block, block.shape[dim] - width, None, axis=dim), axis, forward
        )
        high = lax.ppermute(lax.slice_in_dim(block, 0, width, axis=dim), axis, backward)
        block = jnp.concatenate([low, block, high], axis=dim)
    return block


def column_taps(values, taps):
    width = values.shape[-1]
    wide = jnp.pad(values, ((0, 0), (0, 0), (3, 3)))
    total = taps[0] * wide[..., 0:width]
    for k in range(1, 7):
        total = total + taps[k] * wide[..., k : k + width]
    return total


def row_taps(values, taps):
    count = values.shape[1] - 6
    total = taps[0] * values[:, 0:count]
    for k in range(1, 7):
        total = total + taps[k] * values[:, k : k + count]
    return total


def halve_table(width):
    source = np.arange(width)[:, None]
    target = np.arange(width // 2)[None, :]
    place = source - 2 * target + 1
    table = np.zeros((width, width // 2), np.float32)
    for p in range(4):
        table = table + pyramid_filter[p] * (place == p)
    return jnp.asarray(table, jnp.bfloat16)


def halve_columns(values):
    table = halve_table(values.shape[-1])
    high = values.astype(jnp.bfloat16)
    low = (values - high.astype(jnp.float32)).astype(jnp.bfloat16)
    dims = (((values.ndim - 1,), (0,)), ((), ()))
    return lax.dot_general(high, table, dims, preferred_element_type=jnp.float32) + lax.dot_general(
        low, table, dims, preferred_element_type=jnp.float32
    )


def halve_rows(extended):
    pairs_count = extended.shape[1] // 2
    pairs = extended.reshape(extended.shape[:1] + (pairs_count, 2) + extended.shape[2:])
    even = pairs[:, :, 0]
    odd = pairs[:, :, 1]
    return (
        pyramid_filter[0] * even[:, :-1]
        + pyramid_filter[1] * odd[:, :-1]
        + pyramid_filter[2] * even[:, 1:]
        + pyramid_filter[3] * odd[:, 1:]
    )


def decimate_rim(extended):
    return halve_columns(halve_rows(extended))


def keep_rows(values, first, total):
    places = first + lax.iota(jnp.int32, values.shape[1])
    inside = (places >= 0) & (places < total)
    return jnp.where(inside[None, :, None], values, 0.0)


def smooth_operator(dates):
    clamp = np.zeros((dates, dates), np.float64)
    near = np.zeros((dates, dates), np.float64)
    for t in range(dates):
        for k in range(9):
            clamp[t, min(max(t + k - 4, 0), dates - 1)] += savgol_coeffs[k]
            if 0 <= t + k - 4 < dates:
                near[t, t + k - 4] = gap_weights[k]
    return (clamp.astype(np.float32), near.astype(np.float32))


def smooth_coefficients(clear):
    dates = clear.shape[0]
    clamp, near = smooth_operator(dates)
    weight = 0.1 + 0.9 * clear
    denom = jnp.einsum("su,uxy->sxy", near, weight, precision=lax.Precision.HIGHEST)
    gap = (1.0 - clear) / denom
    fill = near[:, :, None, None] * weight[None, :] * gap[:, None]
    fill = fill + jnp.eye(dates, dtype=jnp.float32)[:, :, None, None] * clear[None, :]
    return jnp.einsum("ts,suxy->tuxy", clamp, fill, precision=lax.Precision.HIGHEST)


def expand(coeff, rows, cols):
    lead = coeff.shape[:-2]
    rm, cm = coeff.shape[-2:]
    grown = jnp.broadcast_to(coeff[..., :, None, :, None], lead + (rm, rows, cm, cols))
    return grown.reshape(lead + (rm * rows, cm * cols))


def smooth(level, coeff, rows, cols):
    values = level.astype(jnp.float32)
    grown = expand(coeff, rows, cols)
    return jnp.sum(grown * values[None], axis=1).astype(jnp.bfloat16)


def local(scenes, resample_taps, clear_mask):
    rows = scenes.shape[2]
    bands = scenes.shape[1]
    band_index = lax.axis_index("row")
    total_rows = rows * lax.axis_size("row")
    ndate = lax.axis_size("date")
    extended = padded(scenes, (("row", 2),), 6)
    clear = clear_mask.astype(jnp.float32)
    coeff = smooth_coefficients(clear)
    mask_rows = clear.shape[1]
    mask_cols = clear.shape[2]
    fine_rows = rows // ndate
    width = scenes.shape[3]
    fine = []
    half = []
    quarter = []
    for b in range(bands):
        source = extended[:, b].astype(jnp.float32)
        across = column_taps(source, resample_taps[0, b])
        resampled_wide = row_taps(across, resample_taps[1, b])
        resampled_wide = keep_rows(resampled_wide, band_index * rows - 3, total_rows)
        half_wide = decimate_rim(resampled_wide)
        half_wide = keep_rows(half_wide, band_index * (rows // 2) - 1, total_rows // 2)
        level_zero = resampled_wide[:, 3 : 3 + rows].astype(jnp.bfloat16)
        level_one = half_wide[:, 1 : 1 + rows // 2].astype(jnp.bfloat16)
        level_two = decimate_rim(half_wide).astype(jnp.bfloat16)
        got = [
            lax.all_to_all(level, "date", split_axis=1, concat_axis=0, tiled=True)
            for level in (level_zero, level_one, level_two)
        ]
        fine.append(smooth(got[0], coeff, fine_rows // mask_rows, width // mask_cols))
        half.append(smooth(got[1], coeff, fine_rows // 2 // mask_rows, width // 2 // mask_cols))
        quarter.append(smooth(got[2], coeff, fine_rows // 4 // mask_rows, width // 4 // mask_cols))
    return tuple((jnp.stack(parts, axis=1) for parts in (fine, half, quarter)))


def solution(mesh):
    in_specs = (P(("groups", "date"), None, "row", None), P(), P("groups", ("row", "date"), None))
    out_specs = (
        P("groups", None, ("row", "date"), None),
        P("groups", None, ("row", "date"), None),
        P("groups", None, ("row", "date"), None),
    )
    return jax.shard_map(local, mesh=mesh, in_specs=in_specs, out_specs=out_specs, check_vma=False)
```

profile of v0, /device:TPU:0, one launch (start us, length us, event | category | flops | bytes accessed | tf_op | source)
XLA Modules:
  0.0 341.9 jit_solution(5171048793330482264)
XLA Ops:
  1.6 2.4 collective-permute-start
  5.4 1.9 fusion.102
  7.2 1.8 fusion.101
  9.1 1.8 fusion.103
  14.0 5.1 %constant_dynamic-update-slice_fusion.1 = bf16[1,4,268,1024]{3,0,2,1:T(2,128)(2,1)S(1)} fusion(bf16[1,4,268,1024]{3,0,2,1:T(2,128)(2,1)S(1)} %constant_dynamic-update-slice_fusion.2, bf16[1,4,256,1024]{3,2,1,0:T(8,128)(2,1)} %param.14), kind=kLoop, calls=%fused_computation.245 | loop fusion | bytes 6291456
  19.2 5.8 %fusion.12 = (f32[1,268,1024]{2,0,1:T(1,128)S(1)}, f32[1,268,1024]{2,0,1:T(1,128)S(1)}, f32[1,268,1024]{2,0,1:T(1,128)}, f32[1,268,1024]{2,0,1:T(1,128)}) fusion(bf16[1,4,268,1024]{3,0,2,1:T(2,128)(2,1)S(1)} %constant_dynamic-update-slice_fusion), kind=kLoop, calls=%fused_computation.39 | loop fusion | flops 1097728 | bytes 6586368 | tf_op jit(solution)/shard_map/convert_element_type | solution.py:138
  25.0 37.0 %multiply_add_fusion = (f32[1,268,1024]{2,0,1:T(1,128)S(1)}, f32[1,268,1024]{2,0,1:T(1,128)S(1)}) fusion(f32[1,268,1024]{2,0,1:T(1,128)S(1)} %get-tuple-element.31, f32[]{:T(128)} %bitcast.66, f32[]{:T(128)} %bitcast.65, f32[]{:T(128)} %bitcast.64, f32[]{:T(128)} %bitcast.62, f32[]{:T(128)} %bitcast.61, f32[]{:T(128)} %bitcast.60, f32[]{:T(128)} %bitcast.58, ...), kind=kLoop, calls=%fused_computation.46 | loop fusion | flops 7135232 | bytes 4390968 | tf_op jit(solution)/shard_map/add | solution.py:31
  62.0 9.8 %broadcast_select_fusion = f32[1,262,1024]{2,0,1:T(1,128)S(1)} fusion(pred[262]{0:T(512)(128)(4,1)S(1)} %fusion.89, f32[1,268,1024]{2,0,1:T(1,128)S(1)} %get-tuple-element.109, f32[]{:T(128)} %bitcast.72, f32[]{:T(128)} %bitcast.71, f32[]{:T(128)} %bitcast.70, f32[]{:T(128)} %bitcast.69, f32[]{:T(128)} %bitcast.68, f32[]{:T(128)} %bitcast.67, f32[]{:T(128)} %bitcast.57), kind=kLoop, calls=%fused_computation.8 | loop fusion | flops 3756032 | bytes 8585506 | tf_op jit(solution)/shard_map/jit(_where)/select_n | solution.py:83
  72.6 2.1 subtract_convert_fusion
  76.0 2.0 reshape.705
  83.2 7.0 %all-to-all-start.11 = ((bf16[8,2,1024]{2,1,0:T(2,128)(2,1)}), bf16[8,2,1024]{2,1,0:T(2,128)(2,1)}, u32[]{:S(2)}, u32[]{:S(2)}) async-start(bf16[8,2,1024]{2,1,0:T(2,128)(2,1)} %reshape.736), calls=%async_computation.11 | async-start | bytes 65536 | tf_op jit(solution)/shard_map/all_to_all | solution.py:148
  90.2 9.8 %broadcast_select_fusion.1 = f32[1,262,1024]{2,0,1:T(1,128)S(1)} fusion(pred[262]{0:T(512)(128)(4,1)S(1)} %fusion.89, f32[1,268,1024]{2,0,1:T(1,128)S(1)} %get-tuple-element.110, f32[]{:T(128)} %bitcast.54, f32[]{:T(128)} %bitcast.53, f32[]{:T(128)} %bitcast.52, f32[]{:T(128)} %bitcast.51, f32[]{:T(128)} %bitcast.50, f32[]{:T(128)} %bitcast.49, f32[]{:T(128)} %bitcast.39), kind=kLoop, calls=%fused_computation.9 | loop fusion | flops 3756032 | bytes 8585506 | tf_op jit(solution)/shard_map/jit(_where)/select_n | solution.py:83
  100.8 2.1 subtract_convert_fusion.1
  105.2 38.9 %multiply_add_fusion.2 = (f32[1,268,1024]{2,0,1:T(1,128)S(1)}, f32[1,268,1024]{2,0,1:T(1,128)S(1)}) fusion(f32[1,268,1024]{2,0,1:T(1,128)S(1)} %copy-done.8, f32[]{:T(128)} %bitcast.30, f32[]{:T(128)} %bitcast.29, f32[]{:T(128)} %bitcast.28, f32[]{:T(128)} %bitcast.26, f32[]{:T(128)} %bitcast.25, f32[]{:T(128)} %bitcast.24, f32[]{:T(128)} %bitcast.22, ...), kind=kLoop, calls=%fused_computation.52 | loop fusion | flops 7135232 | bytes 4390968 | tf_op jit(solution)/shard_map/add | solution.py:31
  144.2 9.6 %broadcast_select_fusion.2 = f32[1,262,1024]{2,0,1:T(1,128)S(1)} fusion(pred[262]{0:T(512)(128)(4,1)S(1)} %fusion.89, f32[1,268,1024]{2,0,1:T(1,128)S(1)} %get-tuple-element.111, f32[]{:T(128)} %bitcast.36, f32[]{:T(128)} %bitcast.35, f32[]{:T(128)} %bitcast.34, f32[]{:T(128)} %bitcast.33, f32[]{:T(128)} %bitcast.32, f32[]{:T(128)} %bitcast.31, f32[]{:T(128)} %bitcast.21), kind=kLoop, calls=%fused_computation.10 | loop fusion | flops 3756032 | bytes 8585506 | tf_op jit(solution)/shard_map/jit(_where)/select_n | solution.py:83
  154.6 2.1 subtract_convert_fusion.2
  158.0 2.0 reshape.703
  162.9 10.4 %broadcast_select_fusion.3 = f32[1,262,1024]{2,0,1:T(1,128)S(1)} fusion(pred[262]{0:T(512)(128)(4,1)S(1)} %fusion.89, f32[1,268,1024]{2,0,1:T(1,128)S(1)} %get-tuple-element.112, f32[]{:T(128)} %bitcast.18, f32[]{:T(128)} %bitcast.17, f32[]{:T(128)} %bitcast.16, f32[]{:T(128)} %bitcast.15, f32[]{:T(128)} %bitcast.14, f32[]{:T(128)} %bitcast.13, f32[]{:T(128)} %bitcast.3), kind=kLoop, calls=%fused_computation.11 | loop fusion | flops 3756032 | bytes 8585506 | tf_op jit(solution)/shard_map/jit(_where)/select_n | solution.py:83
  174.1 2.1 subtract_convert_fusion.3
  179.4 6.0 %all-to-all-start.10 = ((bf16[8,2,1024]{2,1,0:T(2,128)(2,1)}), bf16[8,2,1024]{2,1,0:T(2,128)(2,1)S(1)}, u32[]{:S(2)}, u32[]{:S(2)}) async-start(bf16[8,2,1024]{2,1,0:T(2,128)(2,1)} %reshape.734), calls=%async_computation.10 | async-start | bytes 65536 | tf_op jit(solution)/shard_map/all_to_all | solution.py:148
  187.0 5.1 %all-to-all-done.10 = bf16[8,2,1024]{2,1,0:T(2,128)(2,1)S(1)} async-done(((bf16[8,2,1024]{2,1,0:T(2,128)(2,1)}), bf16[8,2,1024]{2,1,0:T(2,128)(2,1)S(1)}, u32[]{:S(2)}, u32[]{:S(2)}) %all-to-all-start.10) | async-done | bytes 32800 | tf_op jit(solution)/shard_map/all_to_all | solution.py:148
  192.1 3.3 all-to-all-start.9
  197.1 5.0 %all-to-all-done.9 = bf16[8,2,1024]{2,1,0:T(2,128)(2,1)S(1)} async-done(((bf16[8,2,1024]{2,1,0:T(2,128)(2,1)}), bf16[8,2,1024]{2,1,0:T(2,128)(2,1)S(1)}, u32[]{:S(2)}, u32[]{:S(2)}) %all-to-all-start.9) | async-done | bytes 32800 | tf_op jit(solution)/shard_map/all_to_all | solution.py:148
  202.0 3.3 all-to-all-start.8
  207.8 4.3 %all-to-all-done.8 = bf16[8,2,1024]{2,1,0:T(2,128)(2,1)S(1)} async-done(((bf16[8,2,1024]{2,1,0:T(2,128)(2,1)}), bf16[8,2,1024]{2,1,0:T(2,128)(2,1)S(1)}, u32[]{:S(2)}, u32[]{:S(2)}) %all-to-all-start.8) | async-done | bytes 32800 | tf_op jit(solution)/shard_map/all_to_all | solution.py:148
  212.0 3.4 all-to-all-start.7
  217.8 4.9 %all-to-all-done.7 = bf16[8,2,4096]{2,1,0:T(2,128)(2,1)S(1)} async-done(((bf16[8,2,4096]{2,1,0:T(2,128)(2,1)}), bf16[8,2,4096]{2,1,0:T(2,128)(2,1)S(1)}, u32[]{:S(2)}, u32[]{:S(2)}) %all-to-all-start.7) | async-done | bytes 131104 | tf_op jit(solution)/shard_map/all_to_all | solution.py:148
  222.7 3.4 all-to-all-start.6
  228.4 4.9 %all-to-all-done.6 = bf16[8,2,4096]{2,1,0:T(2,128)(2,1)S(1)} async-done(((bf16[8,2,4096]{2,1,0:T(2,128)(2,1)}), bf16[8,2,4096]{2,1,0:T(2,128)(2,1)S(1)}, u32[]{:S(2)}, u32[]{:S(2)}) %all-to-all-start.6) | async-done | bytes 131104 | tf_op jit(solution)/shard_map/all_to_all | solution.py:148
  233.3 3.4 all-to-all-start.5
  239.1 4.9 %all-to-all-done.5 = bf16[8,2,4096]{2,1,0:T(2,128)(2,1)S(1)} async-done(((bf16[8,2,4096]{2,1,0:T(2,128)(2,1)}), bf16[8,2,4096]{2,1,0:T(2,128)(2,1)S(1)}, u32[]{:S(2)}, u32[]{:S(2)}) %all-to-all-start.5) | async-done | bytes 131104 | tf_op jit(solution)/shard_map/all_to_all | solution.py:148
  244.0 3.5 %all-to-all-start.4 = ((bf16[8,2,4096]{2,1,0:T(2,128)(2,1)}), bf16[8,2,4096]{2,1,0:T(2,128)(2,1)S(1)}, u32[]{:S(2)}, u32[]{:S(2)}) async-start(bf16[8,2,4096]{2,1,0:T(2,128)(2,1)} %reshape.722), calls=%async_computation.4 | async-start | bytes 262144 | tf_op jit(solution)/shard_map/all_to_all | solution.py:148
  248.3 3.6 %reduce.31 = bf16[256,1024]{1,0:T(8,128)(2,1)S(1)} reduce(bf16[256,1,1024]{2,1,0:T(2,128)(2,1)S(1)} %slice_bitcast_fusion.23, bf16[]{:T(256)} %broadcast.215), dimensions={1}, to_apply=%slice_bitcast_fusion.23.reduce_sub_computation | reduce | bytes 1048578
  254.8 4.4 %all-to-all-start.3 = ((bf16[8,2,16384]{2,1,0:T(2,128)(2,1)}), bf16[8,2,16384]{2,1,0:T(2,128)(2,1)}, u32[]{:S(2)}, u32[]{:S(2)}) async-start(bf16[8,2,16384]{2,1,0:T(2,128)(2,1)} %reshape.720), calls=%async_computation.3 | async-start | bytes 1048576 | tf_op jit(solution)/shard_map/all_to_all | solution.py:148
  260.6 3.7 %reduce.30 = bf16[256,1024]{1,0:T(8,128)(2,1)S(1)} reduce(bf16[256,1,1024]{2,1,0:T(2,128)(2,1)S(1)} %slice_bitcast_fusion.22, bf16[]{:T(256)} %broadcast.215), dimensions={1}, to_apply=%slice_bitcast_fusion.22.reduce_sub_computation | reduce | bytes 1048578
  266.3 3.6 %all-to-all-done.3 = bf16[8,2,16384]{2,1,0:T(2,128)(2,1)} async-done(((bf16[8,2,16384]{2,1,0:T(2,128)(2,1)}), bf16[8,2,16384]{2,1,0:T(2,128)(2,1)}, u32[]{:S(2)}, u32[]{:S(2)}) %all-to-all-start.3) | async-done | bytes 524320 | tf_op jit(solution)/shard_map/all_to_all | solution.py:148
  269.9 5.5 %all-to-all-start.2 = ((bf16[8,2,16384]{2,1,0:T(2,128)(2,1)}), bf16[8,2,16384]{2,1,0:T(2,128)(2,1)}, u32[]{:S(2)}, u32[]{:S(2)}) async-start(bf16[8,2,16384]{2,1,0:T(2,128)(2,1)} %reshape.718), calls=%async_computation.2 | async-start | bytes 1048576 | tf_op jit(solution)/shard_map/all_to_all | solution.py:148
  276.1 3.6 %reduce.29 = bf16[256,1024]{1,0:T(8,128)(2,1)S(1)} reduce(bf16[256,1,1024]{2,1,0:T(2,128)(2,1)S(1)} %slice_bitcast_fusion.21, bf16[]{:T(256)} %broadcast.215), dimensions={1}, to_apply=%slice_bitcast_fusion.21.reduce_sub_computation | reduce | bytes 1048578
  280.9 3.6 %reduce.28 = bf16[256,1024]{1,0:T(8,128)(2,1)S(1)} reduce(bf16[256,1,1024]{2,1,0:T(2,128)(2,1)S(1)} %slice_bitcast_fusion.20, bf16[]{:T(256)} %broadcast.215), dimensions={1}, to_apply=%slice_bitcast_fusion.20.reduce_sub_computation | reduce | bytes 1048578
  290.4 6.4 %all-to-all-start.1 = ((bf16[8,2,16384]{2,1,0:T(2,128)(2,1)}), bf16[8,2,16384]{2,1,0:T(2,128)(2,1)S(1)}, u32[]{:S(2)}, u32[]{:S(2)}) async-start(bf16[8,2,16384]{2,1,0:T(2,128)(2,1)} %reshape.716), calls=%async_computation.1 | async-start | bytes 1048576 | tf_op jit(solution)/shard_map/all_to_all | solution.py:148
  300.7 3.1 multiply_reduce_fusion.7
  307.4 7.8 %all-to-all-start = ((bf16[8,2,16384]{2,1,0:T(2,128)(2,1)}), bf16[8,2,16384]{2,1,0:T(2,128)(2,1)}, u32[]{:S(2)}, u32[]{:S(2)}) async-start(bf16[8,2,16384]{2,1,0:T(2,128)(2,1)} %reshape.714), calls=%async_computation | async-start | bytes 1048576 | tf_op jit(solution)/shard_map/all_to_all | solution.py:148
  316.0 2.2 reshape.721
  318.2 2.2 reshape.719
  320.5 1.8 reshape.717
  325.7 3.5 %reshape.715 = bf16[256,1,1024]{2,1,0:T(2,128)(2,1)} reshape(bf16[8,2,16384]{2,1,0:T(2,128)(2,1)} %all-to-all-done) | data formatting | bytes 1048576
  329.1 2.3 bitcast_convert_fusion.3
  331.4 6.1 %multiply_reduce_fusion.3 = (bf16[8,8,4,8,128]{4,3,2,1,0:T(8,128)(2,1)}, bf16[8,8,4,8,128]{4,3,2,1,0:T(8,128)(2,1)}, bf16[8,8,4,8,128]{4,3,2,1,0:T(8,128)(2,1)}, bf16[8,8,4,8,128]{4,3,2,1,0:T(8,128)(2,1)}) fusion(f32[8,8,4,8,128]{4,3,2,1,0:T(8,128)S(1)} %bitcast.303, f32[8,8,8,8]{3,2,1,0:T(8,128)S(1)} %copy.75, f32[8,8,4,8,128]{4,3,2,1,0:T(8,128)S(1)} %bitcast.302, ...), kind=kLoop, calls=%fused_computation.3 | loop fusion | flops 15728640 | bytes 6307840 | tf_op jit(solution)/shard_map/reduce_sum | solution.py:118
  (203 shorter events, 67.4 us)
Async XLA Ops:
  1.6 12.3 %collective-permute-start = (bf16[1,4,6,1024]{3,0,2,1:T(2,128)(2,1)S(1)}, bf16[1,4,6,1024]{3,0,2,1:T(2,128)(2,1)S(1)}, u32[]{:S(2)}, u32[]{:S(2)}) collective-permute-start(bf16[1,4,6,1024]{3,0,2,1:T(2,128)(2,1)S(1)} %copy.168), channel_id=1, source_target_pairs={{0,1},{2,3},{4,5},{6,7},{8,9},{10,11},{12,13},{14,15},{16,17},{18,... | collective-permute-start | bytes 147464 | tf_op jit(solution)/shard_map/ppermute | solution.py:18
  4.1 15.0 %collective-permute-start.1 = (bf16[1,4,6,1024]{3,0,2,1:T(2,128)(2,1)S(1)}, bf16[1,4,6,1024]{3,0,2,1:T(2,128)(2,1)S(1)}, u32[]{:S(2)}, u32[]{:S(2)}) collective-permute-start(bf16[1,4,6,1024]{3,0,2,1:T(2,128)(2,1)S(1)} %copy.169), channel_id=1, source_target_pairs={{1,0},{3,2},{5,4},{7,6},{9,8},{11,10},{13,12},{15,14},{17,16},{19,... | collective-permute-start | bytes 147464 | tf_op jit(solution)/shard_map/ppermute | solution.py:21
  72.6 2.1 copy-start
  76.0 3.5 %copy-start.1 = (bf16[512,256]{1,0:T(8,128)(2,1)S(1)}, bf16[512,256]{1,0:T(8,128)(2,1)}, u32[]{:S(2)}) copy-start(bf16[512,256]{1,0:T(8,128)(2,1)} %constant.50.clone) | copy-start | bytes 786436
  83.2 96.2 %all-to-all-start.11 = ((bf16[8,2,1024]{2,1,0:T(2,128)(2,1)}), bf16[8,2,1024]{2,1,0:T(2,128)(2,1)}, u32[]{:S(2)}, u32[]{:S(2)}) async-start(bf16[8,2,1024]{2,1,0:T(2,128)(2,1)} %reshape.736), calls=%async_computation.11 | async-start | bytes 65536 | tf_op jit(solution)/shard_map/all_to_all | solution.py:148
  100.0 2.8 copy-start.2
  103.5 1.7 copy-start.11
  103.8 1.4 copy-start.8
  153.8 2.8 copy-start.4
  173.4 2.8 copy-start.6
  176.8 0.9 copy-start.25
  177.2 8.2 %copy-start.26 = (bf16[1,64,512]{2,0,1:T(2,128)(2,1)S(1)}, bf16[1,64,512]{2,0,1:T(2,128)(2,1)}, u32[]{:S(2)}) copy-start(bf16[1,64,512]{2,0,1:T(2,128)(2,1)} %get-tuple-element.19) | copy-start | bytes 196612
  177.2 8.2 %copy-start.27 = (f32[64,256]{1,0:T(8,128)S(1)}, f32[64,256]{1,0:T(8,128)}, u32[]{:S(2)}) copy-start(f32[64,256]{1,0:T(8,128)} %fusion.83) | copy-start | bytes 196612
  177.8 27.6 %copy-start.10 = (f32[130,512]{1,0:T(8,128)S(1)}, f32[130,512]{1,0:T(8,128)}, u32[]{:S(2)}) copy-start(f32[130,512]{1,0:T(8,128)} %fusion) | copy-start | bytes 798724
  179.4 12.7 %all-to-all-start.10 = ((bf16[8,2,1024]{2,1,0:T(2,128)(2,1)}), bf16[8,2,1024]{2,1,0:T(2,128)(2,1)S(1)}, u32[]{:S(2)}, u32[]{:S(2)}) async-start(bf16[8,2,1024]{2,1,0:T(2,128)(2,1)} %reshape.734), calls=%async_computation.10 | async-start | bytes 65536 | tf_op jit(solution)/shard_map/all_to_all | solution.py:148
  192.1 10.0 %all-to-all-start.9 = ((bf16[8,2,1024]{2,1,0:T(2,128)(2,1)}), bf16[8,2,1024]{2,1,0:T(2,128)(2,1)S(1)}, u32[]{:S(2)}, u32[]{:S(2)}) async-start(bf16[8,2,1024]{2,1,0:T(2,128)(2,1)} %reshape.732), calls=%async_computation.9 | async-start | bytes 65536 | tf_op jit(solution)/shard_map/all_to_all | solution.py:148
  195.7 19.7 %copy-start.12 = (f32[130,512]{1,0:T(8,128)S(1)}, f32[130,512]{1,0:T(8,128)}, u32[]{:S(2)}) copy-start(f32[130,512]{1,0:T(8,128)} %copy-done.11) | copy-start | bytes 798724
  202.0 10.0 %all-to-all-start.8 = ((bf16[8,2,1024]{2,1,0:T(2,128)(2,1)}), bf16[8,2,1024]{2,1,0:T(2,128)(2,1)S(1)}, u32[]{:S(2)}, u32[]{:S(2)}) async-start(bf16[8,2,1024]{2,1,0:T(2,128)(2,1)} %reshape.730), calls=%async_computation.8 | async-start | bytes 65536 | tf_op jit(solution)/shard_map/all_to_all | solution.py:148
  207.8 18.3 %copy-start.13 = (f32[130,512]{1,0:T(8,128)S(1)}, f32[130,512]{1,0:T(8,128)}, u32[]{:S(2)}) copy-start(f32[130,512]{1,0:T(8,128)} %fusion.2) | copy-start | bytes 798724
  212.0 10.7 %all-to-all-start.7 = ((bf16[8,2,4096]{2,1,0:T(2,128)(2,1)}), bf16[8,2,4096]{2,1,0:T(2,128)(2,1)S(1)}, u32[]{:S(2)}, u32[]{:S(2)}) async-start(bf16[8,2,4096]{2,1,0:T(2,128)(2,1)} %reshape.728), calls=%async_computation.7 | async-start | bytes 262144 | tf_op jit(solution)/shard_map/all_to_all | solution.py:148
  222.7 10.7 %copy-start.17 = (bf16[8,2,4096]{2,1,0:T(2,128)(2,1)}, bf16[8,2,4096]{2,1,0:T(2,128)(2,1)S(1)}, u32[]{:S(2)}) copy-start(bf16[8,2,4096]{2,1,0:T(2,128)(2,1)S(1)} %all-to-all-done.7) | copy-start | bytes 393220
  222.7 10.7 %all-to-all-start.6 = ((bf16[8,2,4096]{2,1,0:T(2,128)(2,1)}), bf16[8,2,4096]{2,1,0:T(2,128)(2,1)S(1)}, u32[]{:S(2)}, u32[]{:S(2)}) async-start(bf16[8,2,4096]{2,1,0:T(2,128)(2,1)} %reshape.726), calls=%async_computation.6 | async-start | bytes 262144 | tf_op jit(solution)/shard_map/all_to_all | solution.py:148
  233.3 10.7 %copy-start.19 = (bf16[8,2,4096]{2,1,0:T(2,128)(2,1)}, bf16[8,2,4096]{2,1,0:T(2,128)(2,1)S(1)}, u32[]{:S(2)}) copy-start(bf16[8,2,4096]{2,1,0:T(2,128)(2,1)S(1)} %all-to-all-done.6) | copy-start | bytes 393220
  233.3 10.7 %all-to-all-start.5 = ((bf16[8,2,4096]{2,1,0:T(2,128)(2,1)}), bf16[8,2,4096]{2,1,0:T(2,128)(2,1)S(1)}, u32[]{:S(2)}, u32[]{:S(2)}) async-start(bf16[8,2,4096]{2,1,0:T(2,128)(2,1)} %reshape.724), calls=%async_computation.5 | async-start | bytes 262144 | tf_op jit(solution)/shard_map/all_to_all | solution.py:148
  244.0 4.3 %copy-start.21 = (bf16[8,2,4096]{2,1,0:T(2,128)(2,1)}, bf16[8,2,4096]{2,1,0:T(2,128)(2,1)S(1)}, u32[]{:S(2)}) copy-start(bf16[8,2,4096]{2,1,0:T(2,128)(2,1)S(1)} %all-to-all-done.5) | copy-start | bytes 393220
  244.0 10.8 %all-to-all-start.4 = ((bf16[8,2,4096]{2,1,0:T(2,128)(2,1)}), bf16[8,2,4096]{2,1,0:T(2,128)(2,1)S(1)}, u32[]{:S(2)}, u32[]{:S(2)}) async-start(bf16[8,2,4096]{2,1,0:T(2,128)(2,1)} %reshape.722), calls=%async_computation.4 | async-start | bytes 262144 | tf_op jit(solution)/shard_map/all_to_all | solution.py:148
  251.9 7.3 %copy-start.28 = (s32[8,8,8]{2,1,0:T(8,128)S(1)}, s32[8,8,8]{2,1,0:T(8,128)}, u32[]{:S(2)}) copy-start(s32[8,8,8]{2,1,0:T(8,128)} %param.16) | copy-start | bytes 6148
  251.9 7.3 %copy-start.29 = (f32[8,8,8]{2,0,1:T(8,128)S(1)}, f32[8,8,8]{2,0,1:T(8,128)}, u32[]{:S(2)}) copy-start(f32[8,8,8]{2,0,1:T(8,128)} %multiply_add_fusion.4) | copy-start | bytes 6148
  252.0 7.4 %copy-start.30 = (f32[8,8,8]{2,0,1:T(8,128)S(1)}, f32[8,8,8]{2,0,1:T(8,128)}, u32[]{:S(2)}) copy-start(f32[8,8,8]{2,0,1:T(8,128)} %convolution_divide_fusion) | copy-start | bytes 6148
  252.0 7.4 %copy-start.31 = (f32[8,8,1,1]{1,0,3,2:T(8,128)S(1)}, f32[8,8,1,1]{1,0,3,2:T(8,128)}, u32[]{:S(2)}) copy-start(f32[8,8,1,1]{1,0,3,2:T(8,128)} %constant.62) | copy-start | bytes 772
  252.0 7.4 %copy-start.32 = (f32[8,8]{0,1:T(8,128)S(1)}, f32[8,8]{0,1:T(8,128)}, u32[]{:S(2)}) copy-start(f32[8,8]{0,1:T(8,128)} %constant.63) | copy-start | bytes 772
  253.2 6.7 %copy-start.3 = (f32[1,262,1024]{2,0,1:T(1,128)S(1)}, f32[1,262,1024]{2,0,1:T(1,128)}, u32[]{:S(2)}) copy-start(f32[1,262,1024]{2,0,1:T(1,128)} %copy-done.2) | copy-start | bytes 3219460
  254.8 5.0 %copy-start.23 = (bf16[8,2,4096]{2,1,0:T(2,128)(2,1)}, bf16[8,2,4096]{2,1,0:T(2,128)(2,1)S(1)}, u32[]{:S(2)}) copy-start(bf16[8,2,4096]{2,1,0:T(2,128)(2,1)S(1)} %all-to-all-done.4) | copy-start | bytes 393220
  254.8 15.0 %all-to-all-start.3 = ((bf16[8,2,16384]{2,1,0:T(2,128)(2,1)}), bf16[8,2,16384]{2,1,0:T(2,128)(2,1)}, u32[]{:S(2)}, u32[]{:S(2)}) async-start(bf16[8,2,16384]{2,1,0:T(2,128)(2,1)} %reshape.720), calls=%async_computation.3 | async-start | bytes 1048576 | tf_op jit(solution)/shard_map/all_to_all | solution.py:148
  260.6 4.9 %copy-start.5 = (f32[1,262,1024]{2,0,1:T(1,128)S(1)}, f32[1,262,1024]{2,0,1:T(1,128)}, u32[]{:S(2)}) copy-start(f32[1,262,1024]{2,0,1:T(1,128)} %copy-done.4) | copy-start | bytes 3219460
  265.5 9.8 %copy-start.7 = (f32[1,262,1024]{2,0,1:T(1,128)S(1)}, f32[1,262,1024]{2,0,1:T(1,128)}, u32[]{:S(2)}) copy-start(f32[1,262,1024]{2,0,1:T(1,128)} %copy-done.6) | copy-start | bytes 3219460
  269.9 20.5 %all-to-all-start.2 = ((bf16[8,2,16384]{2,1,0:T(2,128)(2,1)}), bf16[8,2,16384]{2,1,0:T(2,128)(2,1)}, u32[]{:S(2)}, u32[]{:S(2)}) async-start(bf16[8,2,16384]{2,1,0:T(2,128)(2,1)} %reshape.718), calls=%async_computation.2 | async-start | bytes 1048576 | tf_op jit(solution)/shard_map/all_to_all | solution.py:148
  287.8 2.5 copy-start.18
  290.4 7.3 %copy-start.20 = (bf16[8,2,4096]{2,1,0:T(2,128)(2,1)S(1)}, bf16[8,2,4096]{2,1,0:T(2,128)(2,1)}, u32[]{:S(2)}) copy-start(bf16[8,2,4096]{2,1,0:T(2,128)(2,1)} %copy-done.19) | copy-start | bytes 393220
  290.4 17.0 %all-to-all-start.1 = ((bf16[8,2,16384]{2,1,0:T(2,128)(2,1)}), bf16[8,2,16384]{2,1,0:T(2,128)(2,1)S(1)}, u32[]{:S(2)}, u32[]{:S(2)}) async-start(bf16[8,2,16384]{2,1,0:T(2,128)(2,1)} %reshape.716), calls=%async_computation.1 | async-start | bytes 1048576 | tf_op jit(solution)/shard_map/all_to_all | solution.py:148
  297.5 1.2 copy-start.22
  298.6 1.2 copy-start.24
  307.4 18.3 %all-to-all-start = ((bf16[8,2,16384]{2,1,0:T(2,128)(2,1)}), bf16[8,2,16384]{2,1,0:T(2,128)(2,1)}, u32[]{:S(2)}, u32[]{:S(2)}) async-start(bf16[8,2,16384]{2,1,0:T(2,128)(2,1)} %reshape.714), calls=%async_computation | async-start | bytes 1048576 | tf_op jit(solution)/shard_map/all_to_all | solution.py:148
  323.3 1.2 copy-start.9
  337.5 1.4 copy-start.16
  337.5 1.6 copy-start.15
  338.9 1.0 copy-start.14
where the time goes:
time: 348 us; the launch traced here: 342 us
  other arithmetic  180 us (52%)
  starting transfers between devices  61.1 us (18%)
  local copies, waits for them, and re-layouts  55.6 us (16%)
  waiting for transfers between devices  35.1 us (10%)
  matrix products  7.96 us (2%)
    add x2, other arithmetic, column_taps(): total = total + taps[k] * wide[..., k:k + width]  76 us
    all_to_all x12, starting transfers between devices, local(): lax.all_to_all(level, 'date', split_axis=1, concat_axis=0, tiled=True)  57.4 us
    select_n x8, other arithmetic, keep_rows(): return jnp.where(inside[None, :, None], values, 0.0)  39.8 us
    all_to_all x12, waiting for transfers between devices, local(): lax.all_to_all(level, 'date', split_axis=1, concat_axis=0, tiled=True)  35.1 us
    unnamed x99, local copies, waits for them, and re-layouts  31.5 us
    unnamed x12, other arithmetic  23.6 us
    convert_element_type x8, other arithmetic, halve_columns(): low = (values - high.astype(jnp.float32)).astype(jnp.bfloat16)  10.9 us
    reduce_sum x3, other arithmetic, smooth(): return jnp.sum(grown * values[None], axis=1).astype(jnp.bfloat16)  10.4 us
  transfers between devices with their start and end apart: 14, of which 9 were waited for; matrix products, arithmetic and copies ran while one was open for 48% of the time, Pallas kernels for 0%

commit v1 on v0

--- a/solution.py
+++ b/solution.py
@@ -8,6 +8,22 @@
 gap_weights = [math.exp(-((k - 4) ** 2) / 8.0) for k in range(9)]
 savgol_coeffs = [c / 231.0 for c in [-21.0, 14.0, 39.0, 54.0, 59.0, 54.0, 39.0, 14.0, -21.0]]
 pyramid_filter = [0.125, 0.375, 0.375, 0.125]
+
+
+def pairwise_exchange(shard, axis, split, join):
+    ways, here = (lax.axis_size(axis), lax.axis_index(axis))
+    width = shard.shape[split] // ways
+    shape = list(shard.shape)
+    shape[split] = width
+    height = shape[join]
+    shape[join] = height * ways
+    full = jnp.zeros(shape, shard.dtype)
+    for mask in range(ways):
+        part = lax.dynamic_slice_in_dim(shard, (here ^ mask) * width, width, axis=split)
+        if mask:
+            part = lax.ppermute(part, axis, [(d, d ^ mask) for d in range(ways)])
+        full = lax.dynamic_update_slice_in_dim(full, part, (here ^ mask) * height, axis=join)
+    return full
 
 
 def padded(block, sides, width):
@@ -145,8 +161,7 @@
         level_one = half_wide[:, 1 : 1 + rows // 2].astype(jnp.bfloat16)
         level_two = decimate_rim(half_wide).astype(jnp.bfloat16)
         got = [
-            lax.all_to_all(level, "date", split_axis=1, concat_axis=0, tiled=True)
-            for level in (level_zero, level_one, level_two)
+            pairwise_exchange(level, "date", 1, 0) for level in (level_zero, level_one, level_two)
         ]
         fine.append(smooth(got[0], coeff, fine_rows // mask_rows, width // mask_cols))
         half.append(smooth(got[1], coeff, fine_rows // 2 // mask_rows, width // 2 // mask_cols))

time: 348 us -> 336 us (0.966)
  other arithmetic: 180 us -> 89.7 us
  starting transfers between devices: 61.1 us -> 139 us
  local copies, waits for them, and re-layouts: 55.6 us -> 72.8 us
  waiting for transfers between devices: 35.1 us -> 19.7 us
    ppermute x0 -> x84, starting transfers between devices: none -> 135 us  [pairwise_exchange(): part = lax.ppermute(part, axis, [(d, d ^ mask) for d in range(ways)])]
    all_to_all x12 -> x0, starting transfers between devices: 57.4 us -> none  [local(): lax.all_to_all(level, 'date', split_axis=1, concat_axis=0, tiled=True)]
    add x2, other arithmetic: 76 us -> 31.7 us  [column_taps(): total = total + taps[k] * wide[..., k:k + width]]
    all_to_all x12 -> x0, waiting for transfers between devices: 35.1 us -> none  [local(): lax.all_to_all(level, 'date', split_axis=1, concat_axis=0, tiled=True)]
    unnamed x99 -> x102, local copies, waits for them, and re-layouts: 31.5 us -> 0.66 us
    unnamed x12 -> x0, other arithmetic: 23.6 us -> none
    ppermute x0 -> x84, waiting for transfers between devices: none -> 19.7 us  [pairwise_exchange(): part = lax.ppermute(part, axis, [(d, d ^ mask) for d in range(ways)])]
    dynamic_update_slice x0 -> x88, local copies, waits for them, and re-layouts: none -> 16.4 us  [pairwise_exchange(): lax.dynamic_update_slice_in_dim(full, part, (here ^ mask) * height, axis=...]
  transfers between devices with their start and end apart: 14 -> 86, of which waited for: 9 -> 8; matrix products, arithmetic and copies ran while one was open for 48% -> 18% of each run, Pallas kernels for 0% -> 0%
where the time goes in v1:
time: 336 us; the launch traced here: 331 us
  starting transfers between devices  139 us (41%)
  other arithmetic  89.7 us (27%)
  local copies, waits for them, and re-layouts  72.8 us (22%)
  waiting for transfers between devices  19.7 us (6%)
  matrix products  7.45 us (2%)
    ppermute x84, starting transfers between devices, pairwise_exchange(): part = lax.ppermute(part, axis, [(d, d ^ mask) for d in range(ways)])  135 us
    add x2, other arithmetic, column_taps(): total = total + taps[k] * wide[..., k:k + width]  31.7 us
    select_n x8, other arithmetic, keep_rows(): return jnp.where(inside[None, :, None], values, 0.0)  28 us
    ppermute x84, waiting for transfers between devices, pairwise_exchange(): part = lax.ppermute(part, axis, [(d, d ^ mask) for d in range(ways)])  19.7 us
    dynamic_update_slice x88, local copies, waits for them, and re-layouts, pairwise_exchange(): lax.dynamic_update_slice_in_dim(full, part, (here ^ mask) * height, axis=...  16.4 us
    reshape x8, local copies, waits for them, and re-layouts, halve_rows(): extended.reshape(extended.shape[:1] + (pairs_count, 2) + extended.shape[2:])  16 us
    reduce_sum x3, other arithmetic, smooth(): return jnp.sum(grown * values[None], axis=1).astype(jnp.bfloat16)  11.5 us
    convert_element_type x8, other arithmetic, halve_columns(): low = (values - high.astype(jnp.float32)).astype(jnp.bfloat16)  9.8 us
  transfers between devices with their start and end apart: 86, of which 8 were waited for; matrix products, arithmetic and copies ran while one was open for 18% of the time, Pallas kernels for 0%

profile of v1, /device:TPU:0, one launch (start us, length us, event | category | flops | bytes accessed | tf_op | source)
XLA Modules:
  0.0 331.3 jit_solution(13600172435750628874)
XLA Ops:
  1.5 2.4 collective-permute-start
  14.9 2.2 pad_maximum_fusion
  18.9 12.8 %fusion.38 = (f32[1,268,1024]{2,1,0:T(8,128)S(1)}, f32[1,268,1024]{2,1,0:T(8,128)S(1)}) fusion(f32[1,268,1024]{2,1,0:T(8,128)S(1)} %get-tuple-element.32, f32[]{:T(128)} %bitcast.46, f32[]{:T(128)} %bitcast.45, f32[]{:T(128)} %bitcast.44, f32[]{:T(128)} %bitcast.42, f32[]{:T(128)} %bitcast.41, f32[]{:T(128)} %bitcast.40, f32[]{:T(128)} %bitcast.38, ...), kind=kLoop, calls=%fused_computation.84 | loop fusion | flops 7135232 | bytes 4390968 | tf_op jit(solution)/shard_map/add | solution.py:47
  31.7 5.4 %fusion.57 = f32[1,262,1024]{2,1,0:T(8,128)S(1)} fusion(f32[1,268,1024]{2,1,0:T(8,128)S(1)} %get-tuple-element.204, f32[]{:T(128)} %bitcast.69, f32[]{:T(128)} %bitcast.68, f32[]{:T(128)} %bitcast.67, f32[]{:T(128)} %bitcast.66, f32[]{:T(128)} %bitcast.65, f32[]{:T(128)} %bitcast.64, f32[]{:T(128)} %bitcast.54, pred[262]{0:T(512)(128)(4,1)S(1)} %fusion.165), kind=kLoop, calls=%fused_computation.105 | loop fusion | flops 3756032 | bytes 8585506 | tf_op jit(solution)/shard_map/jit(_where)/select_n | solution.py:99
  37.0 2.3 reshape.630
  48.3 6.3 %fusion.64 = f32[1,262,1024]{2,1,0:T(8,128)} fusion(f32[1,268,1024]{2,1,0:T(8,128)S(1)} %get-tuple-element.203, f32[]{:T(128)} %bitcast.52, f32[]{:T(128)} %bitcast.51, f32[]{:T(128)} %bitcast.50, f32[]{:T(128)} %bitcast.49, f32[]{:T(128)} %bitcast.48, f32[]{:T(128)} %bitcast.47, f32[]{:T(128)} %bitcast.37, pred[262]{0:T(512)(128)(4,1)S(1)} %fusion.165), kind=kLoop, calls=%fused_computation.119 | loop fusion | flops 3756032 | bytes 8585506 | tf_op jit(solution)/shard_map/jit(_where)/select_n | solution.py:99
  54.6 2.6 reshape.627
  62.3 18.9 %fusion.14 = (f32[1,268,1024]{2,1,0:T(8,128)S(1)}, f32[1,268,1024]{2,1,0:T(8,128)S(1)}) fusion(f32[1,268,1024]{2,1,0:T(8,128)} %get-tuple-element.34, f32[]{:T(128)} %bitcast.12, f32[]{:T(128)} %bitcast.11, f32[]{:T(128)} %bitcast.10, f32[]{:T(128)} %bitcast.8, f32[]{:T(128)} %bitcast.7, f32[]{:T(128)} %bitcast.6, f32[]{:T(128)} %bitcast.4, f32[]{:T(128)} %bitcast.29, ...), kind=kLoop, calls=%fused_computation.60 | loop fusion | flops 7135232 | bytes 4390968 | tf_op jit(solution)/shard_map/add | solution.py:47
  81.2 6.2 %fusion.71 = f32[1,262,1024]{2,1,0:T(8,128)} fusion(f32[1,268,1024]{2,1,0:T(8,128)S(1)} %get-tuple-element.202, f32[]{:T(128)} %bitcast.35, f32[]{:T(128)} %bitcast.34, f32[]{:T(128)} %bitcast.33, f32[]{:T(128)} %bitcast.32, f32[]{:T(128)} %bitcast.31, f32[]{:T(128)} %bitcast.30, f32[]{:T(128)} %bitcast.20, pred[262]{0:T(512)(128)(4,1)S(1)} %fusion.165), kind=kLoop, calls=%fused_computation.133 | loop fusion | flops 3756032 | bytes 8585506 | tf_op jit(solution)/shard_map/jit(_where)/select_n | solution.py:99
  87.4 3.5 %reshape.624 = f32[1,131,2,1024]{3,0,2,1:T(1,128)} reshape(f32[1,262,1024]{2,1,0:T(8,128)} %fusion.71) | data formatting | bytes 2146304 | tf_op jit(solution)/shard_map/reshape | solution.py:81
  99.8 6.2 %fusion.78 = f32[1,262,1024]{2,1,0:T(8,128)} fusion(f32[1,268,1024]{2,1,0:T(8,128)S(1)} %get-tuple-element.201, f32[]{:T(128)} %bitcast.18, f32[]{:T(128)} %bitcast.17, f32[]{:T(128)} %bitcast.16, f32[]{:T(128)} %bitcast.15, f32[]{:T(128)} %bitcast.14, f32[]{:T(128)} %bitcast.13, f32[]{:T(128)} %bitcast.3, pred[262]{0:T(512)(128)(4,1)S(1)} %fusion.165), kind=kLoop, calls=%fused_computation.147 | loop fusion | flops 3756032 | bytes 8585506 | tf_op jit(solution)/shard_map/jit(_where)/select_n | solution.py:99
  106.0 2.6 reshape.621
  109.4 2.3 subtract_convert_fusion.3
  117.7 2.4 collective-permute-start.79
  121.7 3.0 collective-permute-start.82
  136.9 3.4 %collective-permute-done.72 = bf16[1,8,256]{2,1,0:T(8,128)(2,1)S(1)} collective-permute-done((bf16[1,8,256]{2,1,0:T(8,128)(2,1)S(1)}, bf16[1,8,256]{2,1,0:T(8,128)(2,1)S(1)}, u32[]{:S(2)}, u32[]{:S(2)}) %collective-permute-start.72) | collective-permute-done | bytes 4128 | tf_op jit(solution)/shard_map/ppermute | solution.py:24
  140.3 3.6 %collective-permute-start.84 = (bf16[1,8,256]{2,1,0:T(8,128)(2,1)S(1)}, bf16[1,8,256]{2,1,0:T(8,128)(2,1)S(1)}, u32[]{:S(2)}, u32[]{:S(2)}) collective-permute-start(bf16[1,8,256]{2,1,0:T(8,128)(2,1)S(1)} %get-tuple-element.118), channel_id=1, source_target_pairs={{0,12},{2,14},{4,8},{6,10},{8,4},{10,6},{12,0},{14,2},{1,13},{3,15... | collective-permute-start | bytes 12296 | tf_op jit(solution)/shard_map/ppermute | solution.py:24
  144.0 3.6 %collective-permute-done.73 = bf16[1,8,256]{2,1,0:T(8,128)(2,1)S(1)} collective-permute-done((bf16[1,8,256]{2,1,0:T(8,128)(2,1)S(1)}, bf16[1,8,256]{2,1,0:T(8,128)(2,1)S(1)}, u32[]{:S(2)}, u32[]{:S(2)}) %collective-permute-start.73) | collective-permute-done | bytes 4128 | tf_op jit(solution)/shard_map/ppermute | solution.py:24
  148.4 3.7 %collective-permute-done.74 = bf16[1,8,256]{2,1,0:T(8,128)(2,1)S(1)} collective-permute-done((bf16[1,8,256]{2,1,0:T(8,128)(2,1)S(1)}, bf16[1,8,256]{2,1,0:T(8,128)(2,1)S(1)}, u32[]{:S(2)}, u32[]{:S(2)}) %collective-permute-start.74) | collective-permute-done | bytes 4128 | tf_op jit(solution)/shard_map/ppermute | solution.py:24
  152.1 2.3 collective-permute-start.75
  156.6 3.7 %collective-permute-start.77 = (bf16[1,8,256]{2,1,0:T(8,128)(2,1)S(1)}, bf16[1,8,256]{2,1,0:T(8,128)(2,1)S(1)}, u32[]{:S(2)}, u32[]{:S(2)}) collective-permute-start(bf16[1,8,256]{2,1,0:T(8,128)(2,1)S(1)} %get-tuple-element.125), channel_id=1, source_target_pairs={{0,12},{2,14},{4,8},{6,10},{8,4},{10,6},{12,0},{14,2},{1,13},{3,15... | collective-permute-start | bytes 12296 | tf_op jit(solution)/shard_map/ppermute | solution.py:24
  167.8 3.7 %collective-permute-start.70 = (bf16[1,8,256]{2,1,0:T(8,128)(2,1)S(1)}, bf16[1,8,256]{2,1,0:T(8,128)(2,1)S(1)}, u32[]{:S(2)}, u32[]{:S(2)}) collective-permute-start(bf16[1,8,256]{2,1,0:T(8,128)(2,1)S(1)} %get-tuple-element.132), channel_id=1, source_target_pairs={{0,12},{2,14},{4,8},{6,10},{8,4},{10,6},{12,0},{14,2},{1,13},{3,15... | collective-permute-start | bytes 12296 | tf_op jit(solution)/shard_map/ppermute | solution.py:24
  173.2 3.0 collective-permute-start.60
  179.0 3.7 %collective-permute-start.63 = (bf16[1,8,256]{2,1,0:T(8,128)(2,1)S(1)}, bf16[1,8,256]{2,1,0:T(8,128)(2,1)S(1)}, u32[]{:S(2)}, u32[]{:S(2)}) collective-permute-start(bf16[1,8,256]{2,1,0:T(8,128)(2,1)S(1)} %get-tuple-element.139), channel_id=1, source_target_pairs={{0,12},{2,14},{4,8},{6,10},{8,4},{10,6},{12,0},{14,2},{1,13},{3,15... | collective-permute-start | bytes 12296 | tf_op jit(solution)/shard_map/ppermute | solution.py:24
  184.4 3.0 collective-permute-start.53
  190.8 2.3 multiply_reduce_fusion.11
  198.1 3.7 %collective-permute-start.56 = (bf16[1,16,512]{2,1,0:T(8,128)(2,1)}, bf16[1,16,512]{2,1,0:T(8,128)(2,1)S(1)}, u32[]{:S(2)}, u32[]{:S(2)}) collective-permute-start(bf16[1,16,512]{2,1,0:T(8,128)(2,1)} %get-tuple-element.86), channel_id=1, source_target_pairs={{0,12},{2,14},{4,8},{6,10},{8,4},{10,6},{12,0},{14,2},{1,13},{3,15... | collective-permute-start | bytes 49160 | tf_op jit(solution)/shard_map/ppermute | solution.py:24
  208.7 3.1 collective-permute-start.46
  217.0 3.7 %collective-permute-start.49 = (bf16[1,16,512]{2,1,0:T(8,128)(2,1)S(1)}, bf16[1,16,512]{2,1,0:T(8,128)(2,1)S(1)}, u32[]{:S(2)}, u32[]{:S(2)}) collective-permute-start(bf16[1,16,512]{2,1,0:T(8,128)(2,1)S(1)} %copy-done.47), channel_id=1, source_target_pairs={{0,12},{2,14},{4,8},{6,10},{8,4},{10,6},{12,0},{14,2},{1,13},{3,15... | collective-permute-start | bytes 49160 | tf_op jit(solution)/shard_map/ppermute | solution.py:24
  222.6 3.1 collective-permute-start.39
  225.7 2.3 collective-permute-start.40
  228.7 3.7 %collective-permute-start.42 = (bf16[1,16,512]{2,1,0:T(8,128)(2,1)S(1)}, bf16[1,16,512]{2,1,0:T(8,128)(2,1)S(1)}, u32[]{:S(2)}, u32[]{:S(2)}) collective-permute-start(bf16[1,16,512]{2,1,0:T(8,128)(2,1)S(1)} %copy-done.40), channel_id=1, source_target_pairs={{0,12},{2,14},{4,8},{6,10},{8,4},{10,6},{12,0},{14,2},{1,13},{3,15... | collective-permute-start | bytes 49160 | tf_op jit(solution)/shard_map/ppermute | solution.py:24
  234.3 3.1 collective-permute-start.32
  237.4 2.3 collective-permute-start.33
  240.4 3.7 %collective-permute-start.35 = (bf16[1,16,512]{2,1,0:T(8,128)(2,1)S(1)}, bf16[1,16,512]{2,1,0:T(8,128)(2,1)S(1)}, u32[]{:S(2)}, u32[]{:S(2)}) collective-permute-start(bf16[1,16,512]{2,1,0:T(8,128)(2,1)S(1)} %copy-done.33), channel_id=1, source_target_pairs={{0,12},{2,14},{4,8},{6,10},{8,4},{10,6},{12,0},{14,2},{1,13},{3,15... | collective-permute-start | bytes 49160 | tf_op jit(solution)/shard_map/ppermute | solution.py:24
  248.1 3.1 collective-permute-start.25
  262.4 4.3 %multiply_reduce_fusion.7 = (bf16[8,8,2,8,64]{4,3,2,1,0:T(8,128)(2,1)}, bf16[8,8,2,8,64]{4,3,2,1,0:T(8,128)(2,1)}, bf16[8,8,2,8,64]{4,3,2,1,0:T(8,128)(2,1)}, bf16[8,8,2,8,64]{4,3,2,1,0:T(8,128)(2,1)}) fusion(f32[8,8,2,8,64]{4,3,2,1,0:T(8,128)} %reshape.653, f32[8,8,8,8]{3,2,1,0:T(8,128)S(1)} %copy.50, f32[8,8,2,8,64]{4,3,2,1,0:T(8,128)} %reshape.654, ...), kind=kLoop, calls=%fused_computation.7 | loop fusion | flops 3932160 | bytes 1589248 | tf_op jit(solution)/shard_map/reduce_sum | solution.py:134
  271.3 3.7 %collective-permute-start.28 = (bf16[1,32,1024]{2,1,0:T(8,128)(2,1)}, bf16[1,32,1024]{2,1,0:T(8,128)(2,1)S(1)}, u32[]{:S(2)}, u32[]{:S(2)}) collective-permute-start(bf16[1,32,1024]{2,1,0:T(8,128)(2,1)} %get-tuple-element.46), channel_id=1, source_target_pairs={{0,12},{2,14},{4,8},{6,10},{8,4},{10,6},{12,0},{14,2},{1,13},{3,15... | collective-permute-start | bytes 196616 | tf_op jit(solution)/shard_map/ppermute | solution.py:24
  279.4 3.1 collective-permute-start.18
  283.4 2.3 collective-permute-start.19
  286.5 3.8 %collective-permute-start.21 = (bf16[1,32,1024]{2,1,0:T(8,128)(2,1)S(1)}, bf16[1,32,1024]{2,1,0:T(8,128)(2,1)S(1)}, u32[]{:S(2)}, u32[]{:S(2)}) collective-permute-start(bf16[1,32,1024]{2,1,0:T(8,128)(2,1)S(1)} %copy-done.31), channel_id=1, source_target_pairs={{0,12},{2,14},{4,8},{6,10},{8,4},{10,6},{12,0},{14,2},{1,13},{3,15... | collective-permute-start | bytes 196616 | tf_op jit(solution)/shard_map/ppermute | solution.py:24
  293.1 2.9 collective-permute-done.20
  296.1 4.9 %collective-permute-start.12 = (bf16[1,32,1024]{2,1,0:T(8,128)(2,1)S(1)}, bf16[1,32,1024]{2,1,0:T(8,128)(2,1)S(1)}, u32[]{:S(2)}, u32[]{:S(2)}) collective-permute-start(bf16[1,32,1024]{2,1,0:T(8,128)(2,1)S(1)} %copy-done.26), channel_id=1, source_target_pairs={{0,8},{2,10},{4,12},{6,14},{8,0},{10,2},{12,4},{14,6},{1,9},{3,11}... | collective-permute-start | bytes 196616 | tf_op jit(solution)/shard_map/ppermute | solution.py:24
  302.1 2.3 collective-permute-start.14
  311.5 2.4 collective-permute-start.6
  314.0 2.3 collective-permute-start.7
  320.3 3.1 collective-permute-done.8
  323.6 5.0 %multiply_reduce_fusion.3 = (bf16[8,8,4,8,128]{4,3,2,1,0:T(8,128)(2,1)S(1)}, bf16[8,8,4,8,128]{4,3,2,1,0:T(8,128)(2,1)S(1)}, bf16[8,8,4,8,128]{4,3,2,1,0:T(8,128)(2,1)S(1)}, bf16[8,8,4,8,128]{4,3,2,1,0:T(8,128)(2,1)S(1)}) fusion(f32[8,8,4,8,128]{4,3,2,1,0:T(8,128)S(1)} %bitcast.319, f32[8,8,8,8]{3,2,1,0:T(8,128)S(1)} %copy.50, ...), kind=kLoop, calls=%fused_computation.3 | loop fusion | flops 15728640 | bytes 6307840 | tf_op jit(solution)/shard_map/reduce_sum | solution.py:134
  (438 shorter events, 141.8 us)
Async XLA Ops:
  1.5 13.3 %collective-permute-start = (bf16[1,4,6,1024]{3,2,1,0:T(8,128)(2,1)S(1)}, bf16[1,4,6,1024]{3,2,1,0:T(8,128)(2,1)S(1)}, u32[]{:S(2)}, u32[]{:S(2)}) collective-permute-start(bf16[1,4,6,1024]{3,2,1,0:T(8,128)(2,1)S(1)} %get-tuple-element.35), channel_id=1, source_target_pairs={{0,1},{2,3},{4,5},{6,7},{8,9},{10,11},{12,13},{14,15},{16,17},{18,... | collective-permute-start | bytes 147464 | tf_op jit(solution)/shard_map/ppermute | solution.py:34
  3.9 11.0 %collective-permute-start.1 = (bf16[1,4,6,1024]{3,2,1,0:T(8,128)(2,1)S(1)}, bf16[1,4,6,1024]{3,2,1,0:T(8,128)(2,1)S(1)}, u32[]{:S(2)}, u32[]{:S(2)}) collective-permute-start(bf16[1,4,6,1024]{3,2,1,0:T(8,128)(2,1)S(1)} %get-tuple-element.36), channel_id=1, source_target_pairs={{1,0},{3,2},{5,4},{7,6},{9,8},{11,10},{13,12},{15,14},{17,16},{19,... | collective-permute-start | bytes 147464 | tf_op jit(solution)/shard_map/ppermute | solution.py:37
  117.7 18.9 %collective-permute-start.79 = (bf16[1,8,256]{2,1,0:T(8,128)(2,1)S(1)}, bf16[1,8,256]{2,1,0:T(8,128)(2,1)S(1)}, u32[]{:S(2)}, u32[]{:S(2)}) collective-permute-start(bf16[1,8,256]{2,1,0:T(8,128)(2,1)S(1)} %get-tuple-element.123), channel_id=1, source_target_pairs={{0,2},{2,0},{4,6},{6,4},{8,10},{10,8},{12,14},{14,12},{1,3},{3,1},... | collective-permute-start | bytes 12296 | tf_op jit(solution)/shard_map/ppermute | solution.py:24
  120.1 23.8 %collective-permute-start.80 = (bf16[1,8,256]{2,1,0:T(8,128)(2,1)S(1)}, bf16[1,8,256]{2,1,0:T(8,128)(2,1)S(1)}, u32[]{:S(2)}, u32[]{:S(2)}) collective-permute-start(bf16[1,8,256]{2,1,0:T(8,128)(2,1)S(1)} %get-tuple-element.122), channel_id=1, source_target_pairs={{0,4},{2,6},{4,0},{6,2},{8,12},{10,14},{12,8},{14,10},{1,5},{3,7},... | collective-permute-start | bytes 12296 | tf_op jit(solution)/shard_map/ppermute | solution.py:24
  121.7 25.9 %collective-permute-start.81 = (bf16[1,8,256]{2,1,0:T(8,128)(2,1)S(1)}, bf16[1,8,256]{2,1,0:T(8,128)(2,1)S(1)}, u32[]{:S(2)}, u32[]{:S(2)}) collective-permute-start(bf16[1,8,256]{2,1,0:T(8,128)(2,1)S(1)} %get-tuple-element.121), channel_id=1, source_target_pairs={{0,6},{2,4},{4,2},{6,0},{8,14},{10,12},{12,10},{14,8},{1,7},{3,5},... | collective-permute-start | bytes 12296 | tf_op jit(solution)/shard_map/ppermute | solution.py:24
  121.7 32.8 %collective-permute-start.82 = (bf16[1,8,256]{2,1,0:T(8,128)(2,1)S(1)}, bf16[1,8,256]{2,1,0:T(8,128)(2,1)S(1)}, u32[]{:S(2)}, u32[]{:S(2)}) collective-permute-start(bf16[1,8,256]{2,1,0:T(8,128)(2,1)S(1)} %get-tuple-element.120), channel_id=1, source_target_pairs={{0,8},{2,10},{4,12},{6,14},{8,0},{10,2},{12,4},{14,6},{1,9},{3,11}... | collective-permute-start | bytes 12296 | tf_op jit(solution)/shard_map/ppermute | solution.py:24
  124.7 35.7 %collective-permute-start.83 = (bf16[1,8,256]{2,1,0:T(8,128)(2,1)S(1)}, bf16[1,8,256]{2,1,0:T(8,128)(2,1)S(1)}, u32[]{:S(2)}, u32[]{:S(2)}) collective-permute-start(bf16[1,8,256]{2,1,0:T(8,128)(2,1)S(1)} %get-tuple-element.119), channel_id=1, source_target_pairs={{0,10},{2,8},{4,14},{6,12},{8,2},{10,0},{12,6},{14,4},{1,11},{3,9}... | collective-permute-start | bytes 12296 | tf_op jit(solution)/shard_map/ppermute | solution.py:24
  140.3 21.6 %collective-permute-start.84 = (bf16[1,8,256]{2,1,0:T(8,128)(2,1)S(1)}, bf16[1,8,256]{2,1,0:T(8,128)(2,1)S(1)}, u32[]{:S(2)}, u32[]{:S(2)}) collective-permute-start(bf16[1,8,256]{2,1,0:T(8,128)(2,1)S(1)} %get-tuple-element.118), channel_id=1, source_target_pairs={{0,12},{2,14},{4,8},{6,10},{8,4},{10,6},{12,0},{14,2},{1,13},{3,15... | collective-permute-start | bytes 12296 | tf_op jit(solution)/shard_map/ppermute | solution.py:24
  147.5 17.5 %collective-permute-start.85 = (bf16[1,8,256]{2,1,0:T(8,128)(2,1)S(1)}, bf16[1,8,256]{2,1,0:T(8,128)(2,1)S(1)}, u32[]{:S(2)}, u32[]{:S(2)}) collective-permute-start(bf16[1,8,256]{2,1,0:T(8,128)(2,1)S(1)} %get-tuple-element.117), channel_id=1, source_target_pairs={{0,14},{2,12},{4,10},{6,8},{8,6},{10,4},{12,2},{14,0},{1,15},{3,13... | collective-permute-start | bytes 12296 | tf_op jit(solution)/shard_map/ppermute | solution.py:24
  162.0 9.6 %collective-permute-start.66 = (bf16[1,8,256]{2,1,0:T(8,128)(2,1)S(1)}, bf16[1,8,256]{2,1,0:T(8,128)(2,1)S(1)}, u32[]{:S(2)}, u32[]{:S(2)}) collective-permute-start(bf16[1,8,256]{2,1,0:T(8,128)(2,1)S(1)} %get-tuple-element.136), channel_id=1, source_target_pairs={{0,4},{2,6},{4,0},{6,2},{8,12},{10,14},{12,8},{14,10},{1,5},{3,7},... | collective-permute-start | bytes 12296 | tf_op jit(solution)/shard_map/ppermute | solution.py:24
  163.3 9.4 %collective-permute-start.67 = (bf16[1,8,256]{2,1,0:T(8,128)(2,1)S(1)}, bf16[1,8,256]{2,1,0:T(8,128)(2,1)S(1)}, u32[]{:S(2)}, u32[]{:S(2)}) collective-permute-start(bf16[1,8,256]{2,1,0:T(8,128)(2,1)S(1)} %get-tuple-element.135), channel_id=1, source_target_pairs={{0,6},{2,4},{4,2},{6,0},{8,14},{10,12},{12,10},{14,8},{1,7},{3,5},... | collective-permute-start | bytes 12296 | tf_op jit(solution)/shard_map/ppermute | solution.py:24
  173.1 9.6 %collective-permute-start.59 = (bf16[1,8,256]{2,1,0:T(8,128)(2,1)S(1)}, bf16[1,8,256]{2,1,0:T(8,128)(2,1)S(1)}, u32[]{:S(2)}, u32[]{:S(2)}) collective-permute-start(bf16[1,8,256]{2,1,0:T(8,128)(2,1)S(1)} %get-tuple-element.143), channel_id=1, source_target_pairs={{0,4},{2,6},{4,0},{6,2},{8,12},{10,14},{12,8},{14,10},{1,5},{3,7},... | collective-permute-start | bytes 12296 | tf_op jit(solution)/shard_map/ppermute | solution.py:24
  173.2 10.7 %collective-permute-start.60 = (bf16[1,8,256]{2,1,0:T(8,128)(2,1)S(1)}, bf16[1,8,256]{2,1,0:T(8,128)(2,1)S(1)}, u32[]{:S(2)}, u32[]{:S(2)}) collective-permute-start(bf16[1,8,256]{2,1,0:T(8,128)(2,1)S(1)} %get-tuple-element.142), channel_id=1, source_target_pairs={{0,6},{2,4},{4,2},{6,0},{8,14},{10,12},{12,10},{14,8},{1,7},{3,5},... | collective-permute-start | bytes 12296 | tf_op jit(solution)/shard_map/ppermute | solution.py:24
  183.9 14.2 %collective-permute-start.51 = (bf16[1,16,512]{2,1,0:T(8,128)(2,1)}, bf16[1,16,512]{2,1,0:T(8,128)(2,1)}, u32[]{:S(2)}, u32[]{:S(2)}) collective-permute-start(bf16[1,16,512]{2,1,0:T(8,128)(2,1)} %get-tuple-element.91), channel_id=1, source_target_pairs={{0,2},{2,0},{4,6},{6,4},{8,10},{10,8},{12,14},{14,12},{1,3},{3,1},... | collective-permute-start | bytes 49160 | tf_op jit(solution)/shard_map/ppermute | solution.py:24
  184.3 18.8 %collective-permute-start.52 = (bf16[1,16,512]{2,1,0:T(8,128)(2,1)}, bf16[1,16,512]{2,1,0:T(8,128)(2,1)}, u32[]{:S(2)}, u32[]{:S(2)}) collective-permute-start(bf16[1,16,512]{2,1,0:T(8,128)(2,1)} %get-tuple-element.90), channel_id=1, source_target_pairs={{0,4},{2,6},{4,0},{6,2},{8,12},{10,14},{12,8},{14,10},{1,5},{3,7},... | collective-permute-start | bytes 49160 | tf_op jit(solution)/shard_map/ppermute | solution.py:24
  184.4 21.2 %collective-permute-start.53 = (bf16[1,16,512]{2,1,0:T(8,128)(2,1)}, bf16[1,16,512]{2,1,0:T(8,128)(2,1)}, u32[]{:S(2)}, u32[]{:S(2)}) collective-permute-start(bf16[1,16,512]{2,1,0:T(8,128)(2,1)} %get-tuple-element.89), channel_id=1, source_target_pairs={{0,6},{2,4},{4,2},{6,0},{8,14},{10,12},{12,10},{14,8},{1,7},{3,5},... | collective-permute-start | bytes 49160 | tf_op jit(solution)/shard_map/ppermute | solution.py:24
  187.4 19.9 %collective-permute-start.54 = (bf16[1,16,512]{2,1,0:T(8,128)(2,1)}, bf16[1,16,512]{2,1,0:T(8,128)(2,1)}, u32[]{:S(2)}, u32[]{:S(2)}) collective-permute-start(bf16[1,16,512]{2,1,0:T(8,128)(2,1)} %get-tuple-element.88), channel_id=1, source_target_pairs={{0,8},{2,10},{4,12},{6,14},{8,0},{10,2},{12,4},{14,6},{1,9},{3,11}... | collective-permute-start | bytes 49160 | tf_op jit(solution)/shard_map/ppermute | solution.py:24
  190.0 18.7 %collective-permute-start.55 = (bf16[1,16,512]{2,1,0:T(8,128)(2,1)}, bf16[1,16,512]{2,1,0:T(8,128)(2,1)}, u32[]{:S(2)}, u32[]{:S(2)}) collective-permute-start(bf16[1,16,512]{2,1,0:T(8,128)(2,1)} %get-tuple-element.87), channel_id=1, source_target_pairs={{0,10},{2,8},{4,14},{6,12},{8,2},{10,0},{12,6},{14,4},{1,11},{3,9}... | collective-permute-start | bytes 49160 | tf_op jit(solution)/shard_map/ppermute | solution.py:24
  198.1 15.0 %collective-permute-start.56 = (bf16[1,16,512]{2,1,0:T(8,128)(2,1)}, bf16[1,16,512]{2,1,0:T(8,128)(2,1)S(1)}, u32[]{:S(2)}, u32[]{:S(2)}) collective-permute-start(bf16[1,16,512]{2,1,0:T(8,128)(2,1)} %get-tuple-element.86), channel_id=1, source_target_pairs={{0,12},{2,14},{4,8},{6,10},{8,4},{10,6},{12,0},{14,2},{1,13},{3,15... | collective-permute-start | bytes 49160 | tf_op jit(solution)/shard_map/ppermute | solution.py:24
  203.1 12.7 %collective-permute-start.57 = (bf16[1,16,512]{2,1,0:T(8,128)(2,1)}, bf16[1,16,512]{2,1,0:T(8,128)(2,1)S(1)}, u32[]{:S(2)}, u32[]{:S(2)}) collective-permute-start(bf16[1,16,512]{2,1,0:T(8,128)(2,1)} %get-tuple-element.85), channel_id=1, source_target_pairs={{0,14},{2,12},{4,10},{6,8},{8,6},{10,4},{12,2},{14,0},{1,15},{3,13... | collective-permute-start | bytes 49160 | tf_op jit(solution)/shard_map/ppermute | solution.py:24
  205.6 11.5 %collective-permute-start.44 = (bf16[1,16,512]{2,1,0:T(8,128)(2,1)}, bf16[1,16,512]{2,1,0:T(8,128)(2,1)S(1)}, u32[]{:S(2)}, u32[]{:S(2)}) collective-permute-start(bf16[1,16,512]{2,1,0:T(8,128)(2,1)} %get-tuple-element.99), channel_id=1, source_target_pairs={{0,2},{2,0},{4,6},{6,4},{8,10},{10,8},{12,14},{14,12},{1,3},{3,1},... | collective-permute-start | bytes 49160 | tf_op jit(solution)/shard_map/ppermute | solution.py:24
  207.3 13.4 %collective-permute-start.45 = (bf16[1,16,512]{2,1,0:T(8,128)(2,1)}, bf16[1,16,512]{2,1,0:T(8,128)(2,1)S(1)}, u32[]{:S(2)}, u32[]{:S(2)}) collective-permute-start(bf16[1,16,512]{2,1,0:T(8,128)(2,1)} %get-tuple-element.98), channel_id=1, source_target_pairs={{0,4},{2,6},{4,0},{6,2},{8,12},{10,14},{12,8},{14,10},{1,5},{3,7},... | collective-permute-start | bytes 49160 | tf_op jit(solution)/shard_map/ppermute | solution.py:24
  208.7 13.3 %collective-permute-start.46 = (bf16[1,16,512]{2,1,0:T(8,128)(2,1)}, bf16[1,16,512]{2,1,0:T(8,128)(2,1)S(1)}, u32[]{:S(2)}, u32[]{:S(2)}) collective-permute-start(bf16[1,16,512]{2,1,0:T(8,128)(2,1)} %get-tuple-element.97), channel_id=1, source_target_pairs={{0,6},{2,4},{4,2},{6,0},{8,14},{10,12},{12,10},{14,8},{1,7},{3,5},... | collective-permute-start | bytes 49160 | tf_op jit(solution)/shard_map/ppermute | solution.py:24
  213.0 9.5 %collective-permute-start.47 = (bf16[1,16,512]{2,1,0:T(8,128)(2,1)}, bf16[1,16,512]{2,1,0:T(8,128)(2,1)S(1)}, u32[]{:S(2)}, u32[]{:S(2)}) collective-permute-start(bf16[1,16,512]{2,1,0:T(8,128)(2,1)} %get-tuple-element.96), channel_id=1, source_target_pairs={{0,8},{2,10},{4,12},{6,14},{8,0},{10,2},{12,4},{14,6},{1,9},{3,11}... | collective-permute-start | bytes 49160 | tf_op jit(solution)/shard_map/ppermute | solution.py:24
  222.5 9.9 %collective-permute-start.38 = (bf16[1,16,512]{2,1,0:T(8,128)(2,1)S(1)}, bf16[1,16,512]{2,1,0:T(8,128)(2,1)S(1)}, u32[]{:S(2)}, u32[]{:S(2)}) collective-permute-start(bf16[1,16,512]{2,1,0:T(8,128)(2,1)S(1)} %copy-done.44), channel_id=1, source_target_pairs={{0,4},{2,6},{4,0},{6,2},{8,12},{10,14},{12,8},{14,10},{1,5},{3,7},... | collective-permute-start | bytes 49160 | tf_op jit(solution)/shard_map/ppermute | solution.py:24
  222.6 11.1 %collective-permute-start.39 = (bf16[1,16,512]{2,1,0:T(8,128)(2,1)S(1)}, bf16[1,16,512]{2,1,0:T(8,128)(2,1)S(1)}, u32[]{:S(2)}, u32[]{:S(2)}) collective-permute-start(bf16[1,16,512]{2,1,0:T(8,128)(2,1)S(1)} %copy-done.43), channel_id=1, source_target_pairs={{0,6},{2,4},{4,2},{6,0},{8,14},{10,12},{12,10},{14,8},{1,7},{3,5},... | collective-permute-start | bytes 49160 | tf_op jit(solution)/shard_map/ppermute | solution.py:24
  234.2 10.5 %collective-permute-start.31 = (bf16[1,16,512]{2,1,0:T(8,128)(2,1)S(1)}, bf16[1,16,512]{2,1,0:T(8,128)(2,1)S(1)}, u32[]{:S(2)}, u32[]{:S(2)}) collective-permute-start(bf16[1,16,512]{2,1,0:T(8,128)(2,1)S(1)} %copy-done.37), channel_id=1, source_target_pairs={{0,4},{2,6},{4,0},{6,2},{8,12},{10,14},{12,8},{14,10},{1,5},{3,7},... | collective-permute-start | bytes 49160 | tf_op jit(solution)/shard_map/ppermute | solution.py:24
  234.3 12.2 %collective-permute-start.32 = (bf16[1,16,512]{2,1,0:T(8,128)(2,1)S(1)}, bf16[1,16,512]{2,1,0:T(8,128)(2,1)S(1)}, u32[]{:S(2)}, u32[]{:S(2)}) collective-permute-start(bf16[1,16,512]{2,1,0:T(8,128)(2,1)S(1)} %copy-done.36), channel_id=1, source_target_pairs={{0,6},{2,4},{4,2},{6,0},{8,14},{10,12},{12,10},{14,8},{1,7},{3,5},... | collective-permute-start | bytes 49160 | tf_op jit(solution)/shard_map/ppermute | solution.py:24
  237.4 10.1 %collective-permute-start.33 = (bf16[1,16,512]{2,1,0:T(8,128)(2,1)S(1)}, bf16[1,16,512]{2,1,0:T(8,128)(2,1)S(1)}, u32[]{:S(2)}, u32[]{:S(2)}) collective-permute-start(bf16[1,16,512]{2,1,0:T(8,128)(2,1)S(1)} %copy-done.35), channel_id=1, source_target_pairs={{0,8},{2,10},{4,12},{6,14},{8,0},{10,2},{12,4},{14,6},{1,9},{3,11}... | collective-permute-start | bytes 49160 | tf_op jit(solution)/shard_map/ppermute | solution.py:24
  240.4 11.4 %collective-permute-start.35 = (bf16[1,16,512]{2,1,0:T(8,128)(2,1)S(1)}, bf16[1,16,512]{2,1,0:T(8,128)(2,1)S(1)}, u32[]{:S(2)}, u32[]{:S(2)}) collective-permute-start(bf16[1,16,512]{2,1,0:T(8,128)(2,1)S(1)} %copy-done.33), channel_id=1, source_target_pairs={{0,12},{2,14},{4,8},{6,10},{8,4},{10,6},{12,0},{14,2},{1,13},{3,15... | collective-permute-start | bytes 49160 | tf_op jit(solution)/shard_map/ppermute | solution.py:24
  244.7 13.8 %collective-permute-start.36 = (bf16[1,16,512]{2,1,0:T(8,128)(2,1)S(1)}, bf16[1,16,512]{2,1,0:T(8,128)(2,1)}, u32[]{:S(2)}, u32[]{:S(2)}) collective-permute-start(bf16[1,16,512]{2,1,0:T(8,128)(2,1)S(1)} %get-tuple-element.109), channel_id=1, source_target_pairs={{0,14},{2,12},{4,10},{6,8},{8,6},{10,4},{12,2},{14,0},{1,15},{3,13... | collective-permute-start | bytes 49160 | tf_op jit(solution)/shard_map/ppermute | solution.py:24
  246.5 24.8 %collective-permute-start.23 = (bf16[1,32,1024]{2,1,0:T(8,128)(2,1)}, bf16[1,32,1024]{2,1,0:T(8,128)(2,1)S(1)}, u32[]{:S(2)}, u32[]{:S(2)}) collective-permute-start(bf16[1,32,1024]{2,1,0:T(8,128)(2,1)} %get-tuple-element.51), channel_id=1, source_target_pairs={{0,2},{2,0},{4,6},{6,4},{8,10},{10,8},{12,14},{14,12},{1,3},{3,1},... | collective-permute-start | bytes 196616 | tf_op jit(solution)/shard_map/ppermute | solution.py:24
  247.5 27.5 %collective-permute-start.24 = (bf16[1,32,1024]{2,1,0:T(8,128)(2,1)}, bf16[1,32,1024]{2,1,0:T(8,128)(2,1)}, u32[]{:S(2)}, u32[]{:S(2)}) collective-permute-start(bf16[1,32,1024]{2,1,0:T(8,128)(2,1)} %get-tuple-element.50), channel_id=1, source_target_pairs={{0,4},{2,6},{4,0},{6,2},{8,12},{10,14},{12,8},{14,10},{1,5},{3,7},... | collective-permute-start | bytes 196616 | tf_op jit(solution)/shard_map/ppermute | solution.py:24
  248.1 29.0 %collective-permute-start.25 = (bf16[1,32,1024]{2,1,0:T(8,128)(2,1)}, bf16[1,32,1024]{2,1,0:T(8,128)(2,1)}, u32[]{:S(2)}, u32[]{:S(2)}) collective-permute-start(bf16[1,32,1024]{2,1,0:T(8,128)(2,1)} %get-tuple-element.49), channel_id=1, source_target_pairs={{0,6},{2,4},{4,2},{6,0},{8,14},{10,12},{12,10},{14,8},{1,7},{3,5},... | collective-permute-start | bytes 196616 | tf_op jit(solution)/shard_map/ppermute | solution.py:24
  251.8 26.6 %collective-permute-start.26 = (bf16[1,32,1024]{2,1,0:T(8,128)(2,1)}, bf16[1,32,1024]{2,1,0:T(8,128)(2,1)}, u32[]{:S(2)}, u32[]{:S(2)}) collective-permute-start(bf16[1,32,1024]{2,1,0:T(8,128)(2,1)} %get-tuple-element.48), channel_id=1, source_target_pairs={{0,8},{2,10},{4,12},{6,14},{8,0},{10,2},{12,4},{14,6},{1,9},{3,11}... | collective-permute-start | bytes 196616 | tf_op jit(solution)/shard_map/ppermute | solution.py:24
  258.6 20.8 %collective-permute-start.27 = (bf16[1,32,1024]{2,1,0:T(8,128)(2,1)}, bf16[1,32,1024]{2,1,0:T(8,128)(2,1)}, u32[]{:S(2)}, u32[]{:S(2)}) collective-permute-start(bf16[1,32,1024]{2,1,0:T(8,128)(2,1)} %get-tuple-element.47), channel_id=1, source_target_pairs={{0,10},{2,8},{4,14},{6,12},{8,2},{10,0},{12,6},{14,4},{1,11},{3,9}... | collective-permute-start | bytes 196616 | tf_op jit(solution)/shard_map/ppermute | solution.py:24
  271.3 12.1 %collective-permute-start.28 = (bf16[1,32,1024]{2,1,0:T(8,128)(2,1)}, bf16[1,32,1024]{2,1,0:T(8,128)(2,1)S(1)}, u32[]{:S(2)}, u32[]{:S(2)}) collective-permute-start(bf16[1,32,1024]{2,1,0:T(8,128)(2,1)} %get-tuple-element.46), channel_id=1, source_target_pairs={{0,12},{2,14},{4,8},{6,10},{8,4},{10,6},{12,0},{14,2},{1,13},{3,15... | collective-permute-start | bytes 196616 | tf_op jit(solution)/shard_map/ppermute | solution.py:24
  275.0 10.6 %collective-permute-start.29 = (bf16[1,32,1024]{2,1,0:T(8,128)(2,1)}, bf16[1,32,1024]{2,1,0:T(8,128)(2,1)S(1)}, u32[]{:S(2)}, u32[]{:S(2)}) collective-permute-start(bf16[1,32,1024]{2,1,0:T(8,128)(2,1)} %get-tuple-element.45), channel_id=1, source_target_pairs={{0,14},{2,12},{4,10},{6,8},{8,6},{10,4},{12,2},{14,0},{1,15},{3,13... | collective-permute-start | bytes 196616 | tf_op jit(solution)/shard_map/ppermute | solution.py:24
  278.5 11.8 %collective-permute-start.17 = (bf16[1,32,1024]{2,1,0:T(8,128)(2,1)}, bf16[1,32,1024]{2,1,0:T(8,128)(2,1)S(1)}, u32[]{:S(2)}, u32[]{:S(2)}) collective-permute-start(bf16[1,32,1024]{2,1,0:T(8,128)(2,1)} %get-tuple-element.58), channel_id=1, source_target_pairs={{0,4},{2,6},{4,0},{6,2},{8,12},{10,14},{12,8},{14,10},{1,5},{3,7},... | collective-permute-start | bytes 196616 | tf_op jit(solution)/shard_map/ppermute | solution.py:24
  279.4 12.1 %collective-permute-start.18 = (bf16[1,32,1024]{2,1,0:T(8,128)(2,1)}, bf16[1,32,1024]{2,1,0:T(8,128)(2,1)S(1)}, u32[]{:S(2)}, u32[]{:S(2)}) collective-permute-start(bf16[1,32,1024]{2,1,0:T(8,128)(2,1)} %get-tuple-element.57), channel_id=1, source_target_pairs={{0,6},{2,4},{4,2},{6,0},{8,14},{10,12},{12,10},{14,8},{1,7},{3,5},... | collective-permute-start | bytes 196616 | tf_op jit(solution)/shard_map/ppermute | solution.py:24
  285.7 10.3 %collective-permute-start.20 = (bf16[1,32,1024]{2,1,0:T(8,128)(2,1)S(1)}, bf16[1,32,1024]{2,1,0:T(8,128)(2,1)S(1)}, u32[]{:S(2)}, u32[]{:S(2)}) collective-permute-start(bf16[1,32,1024]{2,1,0:T(8,128)(2,1)S(1)} %copy-done.32), channel_id=1, source_target_pairs={{0,10},{2,8},{4,14},{6,12},{8,2},{10,0},{12,6},{14,4},{1,11},{3,9}... | collective-permute-start | bytes 196616 | tf_op jit(solution)/shard_map/ppermute | solution.py:24
  286.5 9.6 %collective-permute-start.21 = (bf16[1,32,1024]{2,1,0:T(8,128)(2,1)S(1)}, bf16[1,32,1024]{2,1,0:T(8,128)(2,1)S(1)}, u32[]{:S(2)}, u32[]{:S(2)}) collective-permute-start(bf16[1,32,1024]{2,1,0:T(8,128)(2,1)S(1)} %copy-done.31), channel_id=1, source_target_pairs={{0,12},{2,14},{4,8},{6,10},{8,4},{10,6},{12,0},{14,2},{1,13},{3,15... | collective-permute-start | bytes 196616 | tf_op jit(solution)/shard_map/ppermute | solution.py:24
  290.3 10.7 %collective-permute-start.22 = (bf16[1,32,1024]{2,1,0:T(8,128)(2,1)S(1)}, bf16[1,32,1024]{2,1,0:T(8,128)(2,1)S(1)}, u32[]{:S(2)}, u32[]{:S(2)}) collective-permute-start(bf16[1,32,1024]{2,1,0:T(8,128)(2,1)S(1)} %copy-done.30), channel_id=1, source_target_pairs={{0,14},{2,12},{4,10},{6,8},{8,6},{10,4},{12,2},{14,0},{1,15},{3,13... | collective-permute-start | bytes 196616 | tf_op jit(solution)/shard_map/ppermute | solution.py:24
  291.6 10.5 %collective-permute-start.9 = (bf16[1,32,1024]{2,1,0:T(8,128)(2,1)S(1)}, bf16[1,32,1024]{2,1,0:T(8,128)(2,1)S(1)}, u32[]{:S(2)}, u32[]{:S(2)}) collective-permute-start(bf16[1,32,1024]{2,1,0:T(8,128)(2,1)S(1)} %copy-done.29), channel_id=1, source_target_pairs={{0,2},{2,0},{4,6},{6,4},{8,10},{10,8},{12,14},{14,12},{1,3},{3,1},... | collective-permute-start | bytes 196616 | tf_op jit(solution)/shard_map/ppermute | solution.py:24
  292.1 12.3 %collective-permute-start.10 = (bf16[1,32,1024]{2,1,0:T(8,128)(2,1)S(1)}, bf16[1,32,1024]{2,1,0:T(8,128)(2,1)S(1)}, u32[]{:S(2)}, u32[]{:S(2)}) collective-permute-start(bf16[1,32,1024]{2,1,0:T(8,128)(2,1)S(1)} %copy-done.28), channel_id=1, source_target_pairs={{0,4},{2,6},{4,0},{6,2},{8,12},{10,14},{12,8},{14,10},{1,5},{3,7},... | collective-permute-start | bytes 196616 | tf_op jit(solution)/shard_map/ppermute | solution.py:24
  295.9 10.3 %collective-permute-start.11 = (bf16[1,32,1024]{2,1,0:T(8,128)(2,1)S(1)}, bf16[1,32,1024]{2,1,0:T(8,128)(2,1)S(1)}, u32[]{:S(2)}, u32[]{:S(2)}) collective-permute-start(bf16[1,32,1024]{2,1,0:T(8,128)(2,1)S(1)} %copy-done.27), channel_id=1, source_target_pairs={{0,6},{2,4},{4,2},{6,0},{8,14},{10,12},{12,10},{14,8},{1,7},{3,5},... | collective-permute-start | bytes 196616 | tf_op jit(solution)/shard_map/ppermute | solution.py:24
  296.1 11.5 %collective-permute-start.12 = (bf16[1,32,1024]{2,1,0:T(8,128)(2,1)S(1)}, bf16[1,32,1024]{2,1,0:T(8,128)(2,1)S(1)}, u32[]{:S(2)}, u32[]{:S(2)}) collective-permute-start(bf16[1,32,1024]{2,1,0:T(8,128)(2,1)S(1)} %copy-done.26), channel_id=1, source_target_pairs={{0,8},{2,10},{4,12},{6,14},{8,0},{10,2},{12,4},{14,6},{1,9},{3,11}... | collective-permute-start | bytes 196616 | tf_op jit(solution)/shard_map/ppermute | solution.py:24
  307.8 10.3 %collective-permute-start.4 = (bf16[1,32,1024]{2,1,0:T(8,128)(2,1)S(1)}, bf16[1,32,1024]{2,1,0:T(8,128)(2,1)S(1)}, u32[]{:S(2)}, u32[]{:S(2)}) collective-permute-start(bf16[1,32,1024]{2,1,0:T(8,128)(2,1)S(1)} %copy-done.20), channel_id=1, source_target_pairs={{0,6},{2,4},{4,2},{6,0},{8,14},{10,12},{12,10},{14,8},{1,7},{3,5},... | collective-permute-start | bytes 196616 | tf_op jit(solution)/shard_map/ppermute | solution.py:24
  (87 other events, 1158.4 us)
